TPU v7x, 256 devices: a whole 4x4x8 slice. The times are simulated.
256 devices in a mesh: ctx: 32 (over y, z), tp: 8 (over x, core).
Axes of the slice: x: 4, y: 4, z: 8, core: 2. Of those that a mesh axis runs over, the one named last changes fastest.
Arguments:
- residual: bfloat16 [8192, 8192], P('ctx', 'tp'), may hold values from -90 to 90
- hyena_gate: bfloat16 [8192, 8192], P('ctx', 'tp'), may hold values from -6 to 6
- hyena_key: bfloat16 [8192, 8192], P('ctx', 'tp'), may hold values from -6 to 6
- hyena_value: bfloat16 [8192, 8192], P('ctx', 'tp'), may hold values from -6 to 6
- filter_taps: float32 [512, 128], P('tp'), may hold values from -0.45 to 0.45
- norm_gain: float32 [8192], P('tp'), may hold values from 0.5 to 1.5
- att_query: bfloat16 [8192, 8192], P('ctx', 'tp'), may hold values from -180 to 180
- att_key: bfloat16 [8192, 8192], P('ctx', 'tp'), may hold values from -6 to 6
- att_value: bfloat16 [8192, 8192], P('ctx', 'tp'), may hold values from -6 to 6
- doc_lengths: int32 [32], replicated, may hold values from 1 to 768, 8192 in all
Outputs:
- normed: bfloat16 [8192, 8192], P('ctx', 'tp')
- attended: bfloat16 [8192, 8192], P('ctx', 'tp')
Inputs may be any that keep to these rules, and one draw needn't show every extreme that they name: `doc_lengths`: the lengths sum to 8192; the longest document has exactly 768 tokens.
All inputs are finite; a program needn't handle non-finite values.
Results may differ from a plain program's by a relative error of at most 0.0075.
Values may be sent and summed in bfloat16 or wider, within the bound.
No kernel may reach another device: no remote copies, remote signals or barrier semaphores. Data moves between devices by JAX's collectives and lax.ppermute only.
A program may use at most 128 MiB of HBM per device.

v0:
```python
import jax
import jax.numpy as jnp
from jax import lax
from jax.sharding import PartitionSpec as P

D = 8192
HEAD_DIM = 128
REACH = 3
norm_epsilon = 1e-05


def shifted(value, axis, steps):
    count = lax.axis_size(axis)
    first, last = (max(0, -steps), min(count, count - steps))
    return lax.ppermute(value, axis, [(source, source + steps) for source in range(first, last)])


def document_begin(doc_lengths, positions):
    count = doc_lengths.shape[0]
    order = jnp.arange(count, dtype=jnp.int32)
    before = order[None, :] < order[:, None]
    starts = jnp.sum(jnp.where(before, doc_lengths[None, :], 0), axis=1)
    return jnp.max(jnp.where(starts[None, :] <= positions[:, None], starts[None, :], 0), axis=1)


def causal_filter(extended, filter_taps, reach_back, out_rows):
    groups, taps = filter_taps.shape
    channels = extended.shape[1]
    width = channels // groups
    lag_table = (
        jnp.arange(taps, dtype=jnp.int32)[:, None]
        + (taps - 1)
        - jnp.arange(2 * taps - 1, dtype=jnp.int32)[None, :]
    )
    reversed_taps = filter_taps[:, ::-1]
    period = jnp.concatenate([reversed_taps, jnp.zeros((groups, taps), jnp.float32)], axis=1)
    tiled = jnp.tile(period, (1, taps))
    toeplitz = tiled[:, : taps * (2 * taps - 1)].reshape(groups, taps, 2 * taps - 1)
    upper_part = toeplitz.astype(jnp.bfloat16)
    lower_part = (toeplitz - upper_part.astype(jnp.float32)).astype(jnp.bfloat16)
    zero_half = jnp.zeros((), jnp.bfloat16)
    numbers = (((0,), (2,)), ((1,), (0,)))
    results = []
    for block_index in range(out_rows // taps):
        first = block_index * taps
        sources = extended[first : first + 2 * taps - 1].reshape(2 * taps - 1, groups, width)
        limits = reach_back[first : first + taps]
        valid = (lag_table <= limits[:, None])[None]
        kernel_upper = jnp.where(valid, upper_part, zero_half)
        kernel_lower = jnp.where(valid, lower_part, zero_half)
        result = lax.dot_general(sources, kernel_upper, numbers, preferred_element_type=jnp.float32)
        result = result + lax.dot_general(
            sources, kernel_lower, numbers, preferred_element_type=jnp.float32
        )
        results.append(result.transpose(2, 0, 1).reshape(taps, channels))
    return jnp.concatenate(results, axis=0)


def attend_part(query_head, key_head, value_head, visible, scale):
    scores = (
        lax.dot_general(
            query_head, key_head, (((1,), (1,)), ((), ())), preferred_element_type=jnp.float32
        )
        * scale
    )
    scores = jnp.where(visible, scores, jnp.float32(-1e30))
    top = jnp.max(scores, axis=1, keepdims=True)
    expo = jnp.where(visible, jnp.exp(scores - top), jnp.float32(0.0))
    denominator = jnp.sum(expo, axis=1, keepdims=True)
    summed = jnp.dot(expo.astype(jnp.bfloat16), value_head, preferred_element_type=jnp.float32)
    return (summed, top, denominator)


def attend_block(queries, keys, values, visible, scale):
    head_count = queries.shape[1] // HEAD_DIM
    sums, tops, dens = ([], [], [])
    for head_index in range(head_count):
        lower = head_index * HEAD_DIM
        upper = lower + HEAD_DIM
        summed, top, den = attend_part(
            queries[:, lower:upper], keys[:, lower:upper], values[:, lower:upper], visible, scale
        )
        sums.append(summed)
        tops.append(top)
        dens.append(den)
    return (jnp.stack(sums, axis=1), jnp.concatenate(tops, axis=1), jnp.concatenate(dens, axis=1))


def on_device(
    residual,
    hyena_gate,
    hyena_key,
    hyena_value,
    filter_taps,
    norm_gain,
    att_query,
    att_key,
    att_value,
    doc_lengths,
):
    tok_rows = residual.shape[0]
    taps = filter_taps.shape[1]
    shard_index = lax.axis_index("ctx")
    anchor = shard_index * tok_rows
    positions = anchor + jnp.arange(tok_rows, dtype=jnp.int32)
    doc_begin = document_begin(doc_lengths, positions)
    mixed_rows = (hyena_key.astype(jnp.float32) * hyena_value.astype(jnp.float32)).astype(
        jnp.bfloat16
    )
    rim_rows = shifted(mixed_rows[tok_rows - (taps - 1) :], "ctx", 1)
    key_pair = jnp.stack([att_key, att_value])
    previous = shifted(key_pair, "ctx", 1)
    later_query = shifted(att_query, "ctx", -2)
    key_rows = jnp.concatenate([previous[0], att_key], axis=0)
    value_rows = jnp.concatenate([previous[1], att_value], axis=0)
    window = key_rows.shape[0]
    key_pos = anchor - tok_rows + jnp.arange(window, dtype=jnp.int32)
    scale = jnp.float32(1.0 / HEAD_DIM**0.5)
    far_pos = positions + 2 * tok_rows
    far_begin = document_begin(doc_lengths, far_pos)
    far_visible = (key_pos[None, :] <= far_pos[:, None]) & (key_pos[None, :] >= far_begin[:, None])
    far_sum, far_top, far_den = attend_block(later_query, key_rows, value_rows, far_visible, scale)
    far_packet = (far_sum.astype(jnp.bfloat16), far_top, far_den)
    far_packet, mixed_rows = lax.optimization_barrier((far_packet, mixed_rows))
    far_sum, far_top, far_den = shifted(far_packet, "ctx", 2)
    extended = jnp.concatenate([rim_rows, mixed_rows], axis=0)
    filtered = causal_filter(extended, filter_taps, positions - doc_begin, tok_rows)
    hidden = residual.astype(jnp.float32) + hyena_gate.astype(jnp.float32) * filtered
    local_sum = jnp.sum(hidden * hidden, axis=1)
    mean_square = lax.psum(local_sum, "tp") / D
    normed = (hidden * lax.rsqrt(mean_square + norm_epsilon)[:, None] * norm_gain[None, :]).astype(
        jnp.bfloat16
    )
    visible = (key_pos[None, :] <= positions[:, None]) & (key_pos[None, :] >= doc_begin[:, None])
    near_sum, near_top, near_den = attend_block(att_query, key_rows, value_rows, visible, scale)
    far_top = jnp.where(far_den > 0, far_top, jnp.float32(-1e30))
    top = jnp.maximum(near_top, far_top)
    near_scale = jnp.exp(near_top - top)
    far_scale = jnp.exp(far_top - top)
    denominator = near_den * near_scale + far_den * far_scale
    summed = near_sum * near_scale[:, :, None] + far_sum.astype(jnp.float32) * far_scale[:, :, None]
    attended = (summed / denominator[:, :, None]).astype(jnp.bfloat16).reshape(tok_rows, -1)
    return (normed, attended)


def solution(mesh):
    placed = (
        P("ctx", "tp"),
        P("ctx", "tp"),
        P("ctx", "tp"),
        P("ctx", "tp"),
        P("tp", None),
        P("tp"),
        P("ctx", "tp"),
        P("ctx", "tp"),
        P("ctx", "tp"),
        P(),
    )
    return jax.shard_map(
        on_device,
        mesh=mesh,
        in_specs=placed,
        out_specs=(P("ctx", "tp"), P("ctx", "tp")),
        check_vma=False,
    )
```

profile of v0, /device:TPU:32, one launch (start us, length us, event | category | flops | bytes accessed | tf_op | source)
XLA Modules:
  0.0 137.4 jit_solution(9986038495159426855)
XLA Ops:
  0.6 1.4 %multiply_convert_fusion.1 = bf16[256,1024]{1,0:T(8,128)(2,1)S(1)} fusion(bf16[256,1024]{1,0:T(8,128)(2,1)} %param.13, bf16[256,1024]{1,0:T(8,128)(2,1)} %param.12), kind=kLoop, calls=%fused_computation.141 | loop fusion | flops 1048576 | bytes 1572864 | tf_op jit(solution)/shard_map/convert_element_type | solution.py:107
  2.8 3.8 %collective-permute-start = (bf16[127,1024]{1,0:T(8,128)(2,1)}, bf16[127,1024]{1,0:T(8,128)(2,1)S(1)}, u32[]{:S(2)}, u32[]{:S(2)}) collective-permute-start(bf16[127,1024]{1,0:T(8,128)(2,1)} %slice.176), channel_id=1, source_target_pairs={{0,8},{8,16},{16,24},{24,32},{32,40},{40,48},{48,56},{56,64},{64,7... | collective-permute-start | bytes 780296 | tf_op jit(solution)/shard_map/ppermute | solution.py:15
  6.6 1.3 collective-permute-start.2
  7.9 2.3 %pad_maximum_fusion = bf16[2,256,1024]{2,1,0:T(8,128)(2,1)} fusion(bf16[1,256,1024]{2,1,0:T(8,128)(2,1)} %bitcast.185, bf16[1,256,1024]{2,1,0:T(8,128)(2,1)} %bitcast.186), kind=kLoop, calls=%fused_computation.135 | loop fusion | flops 524288 | bytes 2097152 | tf_op jit(solution)/shard_map/stack | solution.py:111
  10.2 4.4 %collective-permute-start.1 = (bf16[2,256,1024]{2,1,0:T(8,128)(2,1)}, bf16[2,256,1024]{2,1,0:T(8,128)(2,1)S(1)}, u32[]{:S(2)}, u32[]{:S(2)}) collective-permute-start(bf16[2,256,1024]{2,1,0:T(8,128)(2,1)} %pad_maximum_fusion), channel_id=1, source_target_pairs={{0,8},{8,16},{16,24},{24,32},{32,40},{40,48},{48,56},{56,64},{64,7... | collective-permute-start | bytes 3145736 | tf_op jit(solution)/shard_map/ppermute | solution.py:15
  15.5 4.7 %copy.60 = f32[8,8,128,256]{3,1,2,0:T(8,128)S(1)} copy(f32[8,8,128,256]{3,2,1,0:T(8,128)S(1)} %bitcast.187) | data formatting | bytes 16777216
  20.2 3.7 %slice.215 = f32[64,32640]{1,0:T(8,128)} slice(f32[64,32768]{1,0:T(8,128)S(1)} %bitcast.188), slice={[0:64], [0:32640]} | slice | bytes 16711680 | tf_op jit(solution)/shard_map/slice | solution.py:38
  24.0 16.0 %reshape.128 = f32[64,128,255]{2,1,0:T(8,128)} reshape(f32[64,32640]{1,0:T(8,128)} %slice.215) | data formatting | bytes 16711680 | tf_op jit(solution)/shard_map/reshape | solution.py:38
  40.4 1.2 fusion.262
  59.2 1.4 fusion.93
  63.4 6.0 %collective-permute-start.3 = (f32[256,8]{0,1:T(8,128)S(1)}, f32[256,8]{0,1:T(8,128)S(1)}, u32[]{:S(2)}, u32[]{:S(2)}) collective-permute-start(f32[256,8]{0,1:T(8,128)S(1)} %concatenate.30), channel_id=1, source_target_pairs={{0,16},{8,24},{16,32},{24,40},{32,48},{40,56},{48,64},{56,72},{64,... | collective-permute-start | bytes 24584 | tf_op jit(solution)/shard_map/ppermute | solution.py:15
  69.4 4.5 %collective-permute-start.4 = (f32[256,8]{0,1:T(8,128)}, f32[256,8]{0,1:T(8,128)S(1)}, u32[]{:S(2)}, u32[]{:S(2)}) collective-permute-start(f32[256,8]{0,1:T(8,128)} %concatenate.29), channel_id=1, source_target_pairs={{0,16},{8,24},{16,32},{24,40},{32,48},{40,56},{48,64},{56,72},{64,... | collective-permute-start | bytes 24584 | tf_op jit(solution)/shard_map/ppermute | solution.py:15
  73.9 2.0 %fusion.263 = (f32[256]{0:T(256)S(1)}, f32[256,512]{0,1:T(8,128)}) fusion(bf16[512,128]{1,0:T(8,128)(2,1)} %copy-done.12, bf16[256,1024]{1,0:T(8,128)(2,1)} %param.16, s32[256]{0:T(256)S(1)} %get-tuple-element.30, s32[256]{0:T(256)S(1)} %iota_add_fusion.1, s32[512]{0:T(512)S(1)} %iota_add_fusion), kind=kOutput, calls=%fused_computation.316 | convolution fusion | flops 34340608 | bytes 726016 | tf_op jit(solution)/shard_map/dot_general | solution.py:61
  77.1 1.2 copy.39
  78.3 6.1 %collective-permute-start.5 = (bf16[256,8,128]{2,0,1:T(8,128)(2,1)}, bf16[256,8,128]{2,0,1:T(8,128)(2,1)}, u32[]{:S(2)}, u32[]{:S(2)}) collective-permute-start(bf16[256,8,128]{2,0,1:T(8,128)(2,1)} %copy-done.14), channel_id=1, source_target_pairs={{0,16},{8,24},{16,32},{24,40},{32,48},{40,56},{48,64},{56,72},{64,... | collective-permute-start | bytes 1572872 | tf_op jit(solution)/shard_map/ppermute | solution.py:15
  84.4 7.0 %fusion = f32[64,16,128]{2,1,0:T(8,128)S(1)} fusion(bf16[255,64,16]{0,2,1:T(8,128)(2,1)S(1)} %bitcast.191, pred[128,255]{1,0:T(8,128)(4,1)S(1)} %get-tuple-element.42, f32[64,128,255]{2,1,0:T(8,128)} %reshape.128), kind=kOutput, calls=%fused_computation.1 | convolution fusion | flops 77291520 | bytes 9435008 | tf_op jit(solution)/shard_map/dot_general | solution.py:52
  91.4 5.4 %fusion.51 = f32[64,16,128]{2,1,0:T(8,128)} fusion(f32[64,16,128]{2,1,0:T(8,128)S(1)} %fusion, bf16[255,64,16]{0,2,1:T(8,128)(2,1)S(1)} %bitcast.192, pred[128,255]{1,0:T(8,128)(4,1)S(1)} %get-tuple-element.42, f32[64,128,255]{2,1,0:T(8,128)} %reshape.128), kind=kOutput, calls=%fused_computation.94 | convolution fusion | flops 71155712 | bytes 9959296 | tf_op jit(solution)/shard_map/dot_general | solution.py:51
  96.8 2.1 %copy.41 = f32[128,1024]{1,0:T(8,128)} copy(f32[128,1024]{0,1:T(8,128)} %bitcast.194) | data formatting | bytes 1048576 | tf_op jit(solution)/shard_map/reshape | solution.py:55
  98.8 7.0 %fusion.4 = f32[64,16,128]{2,1,0:T(8,128)S(1)} fusion(bf16[255,64,16]{0,2,1:T(8,128)(2,1)S(1)} %bitcast.189, pred[128,255]{1,0:T(8,128)(4,1)S(1)} %get-tuple-element.41, f32[64,128,255]{2,1,0:T(8,128)} %reshape.128), kind=kOutput, calls=%fused_computation.5 | convolution fusion | flops 77291520 | bytes 9435008 | tf_op jit(solution)/shard_map/dot_general | solution.py:52
  105.8 4.6 %fusion.48 = f32[64,16,128]{2,1,0:T(8,128)S(1)} fusion(f32[64,16,128]{2,1,0:T(8,128)S(1)} %fusion.4, bf16[255,64,16]{0,2,1:T(8,128)(2,1)S(1)} %bitcast.190, pred[128,255]{1,0:T(8,128)(4,1)S(1)} %get-tuple-element.41, f32[64,128,255]{2,1,0:T(8,128)} %reshape.128), kind=kOutput, calls=%fused_computation.93 | convolution fusion | flops 71155712 | bytes 9959296 | tf_op jit(solution)/shard_map/dot_general | solution.py:51
  111.4 1.9 %multiply_reduce_fusion = f32[256]{0:T(256)S(1)} fusion(f32[128,1024]{1,0:T(8,128)} %copy.41, f32[128,1024]{1,0:T(8,128)} %copy.40, bf16[256,1024]{1,0:T(8,128)(2,1)} %param.11, bf16[256,1024]{1,0:T(8,128)(2,1)} %param.10), kind=kLoop, calls=%fused_computation.140 | loop fusion | flops 1834752 | bytes 2098176 | tf_op jit(solution)/shard_map/reduce_sum | solution.py:129
  113.2 12.9 %psum.7 = f32[256]{0:T(256)S(1)} all-reduce(f32[256]{0:T(256)S(1)} %multiply_reduce_fusion), channel_id=1, replica_groups=mesh['ctx'=32,'tp'=8] {'tp'}, use_global_device_ids=true, to_apply=%region_20.21 | all-reduce | flops 256 | bytes 2048 | tf_op jit(solution)/shard_map/psum | solution.py:130
  126.6 2.6 %multiply_convert_fusion = bf16[256,1024]{1,0:T(8,128)(2,1)} fusion(f32[1024]{0:T(1024)S(1)} %copy-done.15, f32[256]{0:T(256)S(1)} %add_rsqrt_fusion, f32[128,1024]{1,0:T(8,128)} %copy.41, f32[128,1024]{1,0:T(8,128)} %copy.40, bf16[256,1024]{1,0:T(8,128)(2,1)} %param.11, bf16[256,1024]{1,0:T(8,128)(2,1)} %param.10), kind=kLoop, calls=%fused_computation.139 | loop fusion | flops 2097152 | bytes 2626560 | tf_op jit(solution)/shard_map/convert_element_type | solution.py:131
  134.1 2.1 %divide_convert_fusion = bf16[256,8,128]{2,0,1:T(8,128)(2,1)S(1)} fusion(bf16[256,8,128]{2,0,1:T(8,128)(2,1)} %collective-permute-done.5, f32[256,8,128]{2,0,1:T(8,128)} %copy-done.7, f32[256,8]{0,1:T(8,128)S(1)} %get-tuple-element.32, f32[256,8]{0,1:T(8,128)S(1)} %get-tuple-element.34, f32[256,8]{0,1:T(8,128)S(1)} %get-tuple-element.33), kind=kLoop, calls=%fused_computation.138 | loop fusion | flops 1572864 | bytes 2121728 | tf_op jit(solution)/shard_map/convert_element_type | solution.py:142
  (96 shorter events, 30.8 us)
Async XLA Ops:
  0.6 14.1 %copy-start.13 = (f32[64,128]{1,0:T(8,128)S(1)}, f32[64,128]{1,0:T(8,128)}, u32[]{:S(2)}) copy-start(f32[64,128]{1,0:T(8,128)} %param.14) | copy-start | bytes 98308
  2.8 73.1 %collective-permute-start = (bf16[127,1024]{1,0:T(8,128)(2,1)}, bf16[127,1024]{1,0:T(8,128)(2,1)S(1)}, u32[]{:S(2)}, u32[]{:S(2)}) collective-permute-start(bf16[127,1024]{1,0:T(8,128)(2,1)} %slice.176), channel_id=1, source_target_pairs={{0,8},{8,16},{16,24},{24,32},{32,40},{40,48},{48,56},{56,64},{64,7... | collective-permute-start | bytes 780296 | tf_op jit(solution)/shard_map/ppermute | solution.py:15
  6.6 40.6 %collective-permute-start.2 = (bf16[256,1024]{1,0:T(8,128)(2,1)}, bf16[256,1024]{1,0:T(8,128)(2,1)}, u32[]{:S(2)}, u32[]{:S(2)}) collective-permute-start(bf16[256,1024]{1,0:T(8,128)(2,1)} %param.16), channel_id=1, source_target_pairs={{16,0},{24,8},{32,16},{40,24},{48,32},{56,40},{64,48},{72,56},{80,... | collective-permute-start | bytes 1572872 | tf_op jit(solution)/shard_map/ppermute | solution.py:15
  10.2 30.1 %collective-permute-start.1 = (bf16[2,256,1024]{2,1,0:T(8,128)(2,1)}, bf16[2,256,1024]{2,1,0:T(8,128)(2,1)S(1)}, u32[]{:S(2)}, u32[]{:S(2)}) collective-permute-start(bf16[2,256,1024]{2,1,0:T(8,128)(2,1)} %pad_maximum_fusion), channel_id=1, source_target_pairs={{0,8},{8,16},{16,24},{24,32},{32,40},{40,48},{48,56},{56,64},{64,7... | collective-permute-start | bytes 3145736 | tf_op jit(solution)/shard_map/ppermute | solution.py:15
  24.0 16.0 %copy-start.16 = (s32[32]{0:T(128)S(1)}, s32[32]{0:T(128)}, u32[]{:S(2)}) copy-start(s32[32]{0:T(128)} %param.19) | copy-start | bytes 388
  24.0 16.5 %copy-start.1 = (bf16[256,1024]{1,0:T(8,128)(2,1)S(1)}, bf16[256,1024]{1,0:T(8,128)(2,1)}, u32[]{:S(2)}) copy-start(bf16[256,1024]{1,0:T(8,128)(2,1)} %param.17) | copy-start | bytes 1572868
  40.0 2.8 %copy-start.9 = (bf16[256,1024]{1,0:T(8,128)(2,1)S(1)}, bf16[256,1024]{1,0:T(8,128)(2,1)}, u32[]{:S(2)}) copy-start(bf16[256,1024]{1,0:T(8,128)(2,1)} %param.16) | copy-start | bytes 1572868
  40.3 4.7 %copy-start = (bf16[256,1024]{1,0:T(8,128)(2,1)S(1)}, bf16[256,1024]{1,0:T(8,128)(2,1)}, u32[]{:S(2)}) copy-start(bf16[256,1024]{1,0:T(8,128)(2,1)} %param.18) | copy-start | bytes 1572868
  45.1 13.0 %copy-start.12 = (bf16[512,128]{1,0:T(8,128)(2,1)}, bf16[512,128]{1,0:T(8,128)(2,1)S(1)}, u32[]{:S(2)}) copy-start(bf16[512,128]{1,0:T(8,128)(2,1)S(1)} %get-tuple-element.76) | copy-start | bytes 393220
  45.1 15.5 %copy-start.10 = (bf16[512,128]{1,0:T(8,128)(2,1)}, bf16[512,128]{1,0:T(8,128)(2,1)S(1)}, u32[]{:S(2)}) copy-start(bf16[512,128]{1,0:T(8,128)(2,1)S(1)} %get-tuple-element.75) | copy-start | bytes 393220
  61.0 1.1 copy-start.14
  63.4 70.6 %collective-permute-start.3 = (f32[256,8]{0,1:T(8,128)S(1)}, f32[256,8]{0,1:T(8,128)S(1)}, u32[]{:S(2)}, u32[]{:S(2)}) collective-permute-start(f32[256,8]{0,1:T(8,128)S(1)} %concatenate.30), channel_id=1, source_target_pairs={{0,16},{8,24},{16,32},{24,40},{32,48},{40,56},{48,64},{56,72},{64,... | collective-permute-start | bytes 24584 | tf_op jit(solution)/shard_map/ppermute | solution.py:15
  69.4 64.6 %collective-permute-start.4 = (f32[256,8]{0,1:T(8,128)}, f32[256,8]{0,1:T(8,128)S(1)}, u32[]{:S(2)}, u32[]{:S(2)}) collective-permute-start(f32[256,8]{0,1:T(8,128)} %concatenate.29), channel_id=1, source_target_pairs={{0,16},{8,24},{16,32},{24,40},{32,48},{40,56},{48,64},{56,72},{64,... | collective-permute-start | bytes 24584 | tf_op jit(solution)/shard_map/ppermute | solution.py:15
  78.3 55.7 %collective-permute-start.5 = (bf16[256,8,128]{2,0,1:T(8,128)(2,1)}, bf16[256,8,128]{2,0,1:T(8,128)(2,1)}, u32[]{:S(2)}, u32[]{:S(2)}) collective-permute-start(bf16[256,8,128]{2,0,1:T(8,128)(2,1)} %copy-done.14), channel_id=1, source_target_pairs={{0,16},{8,24},{16,32},{24,40},{32,48},{40,56},{48,64},{56,72},{64,... | collective-permute-start | bytes 1572872 | tf_op jit(solution)/shard_map/ppermute | solution.py:15
  110.4 16.2 %copy-start.15 = (f32[1024]{0:T(1024)S(1)}, f32[1024]{0:T(1024)}, u32[]{:S(2)}) copy-start(f32[1024]{0:T(1024)} %param.15) | copy-start | bytes 12292
  110.4 18.8 %copy-start.2 = (f32[256,512]{0,1:T(8,128)S(1)}, f32[256,512]{0,1:T(8,128)}, u32[]{:S(2)}) copy-start(f32[256,512]{0,1:T(8,128)} %get-tuple-element.62) | copy-start | bytes 1572868
  111.4 18.2 %copy-start.3 = (f32[256,512]{0,1:T(8,128)S(1)}, f32[256,512]{0,1:T(8,128)}, u32[]{:S(2)}) copy-start(f32[256,512]{0,1:T(8,128)} %get-tuple-element.64) | copy-start | bytes 1572868
  126.2 3.9 %copy-start.4 = (f32[256,512]{0,1:T(8,128)S(1)}, f32[256,512]{0,1:T(8,128)}, u32[]{:S(2)}) copy-start(f32[256,512]{0,1:T(8,128)} %get-tuple-element.66) | copy-start | bytes 1572868
  126.6 3.9 %copy-start.5 = (f32[256,512]{0,1:T(8,128)S(1)}, f32[256,512]{0,1:T(8,128)}, u32[]{:S(2)}) copy-start(f32[256,512]{0,1:T(8,128)} %get-tuple-element.68) | copy-start | bytes 1572868
  126.6 4.3 %copy-start.6 = (f32[256,512]{0,1:T(8,128)S(1)}, f32[256,512]{0,1:T(8,128)}, u32[]{:S(2)}) copy-start(f32[256,512]{0,1:T(8,128)} %get-tuple-element.70) | copy-start | bytes 1572868
  129.2 2.1 %copy-start.8 = (f32[256,512]{0,1:T(8,128)S(1)}, f32[256,512]{0,1:T(8,128)}, u32[]{:S(2)}) copy-start(f32[256,512]{0,1:T(8,128)} %get-tuple-element.74) | copy-start | bytes 1572868
  130.9 1.7 %copy-start.11 = (bf16[512,128]{1,0:T(8,128)(2,1)S(1)}, bf16[512,128]{1,0:T(8,128)(2,1)}, u32[]{:S(2)}) copy-start(bf16[512,128]{1,0:T(8,128)(2,1)} %copy-done.10) | copy-start | bytes 393220
  133.0 1.0 copy-start.7
where the time goes:
time: 138 us; the launch traced here: 137 us
  matrix products  49.2 us (36%)
  local copies, waits for them, and re-layouts  34.2 us (25%)
  starting transfers between devices  26.1 us (19%)
  other arithmetic  13.9 us (10%)
  blocking collectives  12.9 us (9%)
    ppermute x6, starting transfers between devices, shifted(): lax.ppermute(value, axis, [(source, source + steps) for source in range(f...  26.1 us
    dot_general x16, matrix products, attend_part(): lax.dot_general(query_head, key_head, (((1,), (1,)), ((), ())), preferred...  18.7 us
    reshape x1, local copies, waits for them, and re-layouts, causal_filter(): tiled[:, :taps * (2 * taps - 1)].reshape(groups, taps, 2 * taps - 1)  16 us
    dot_general x2, matrix products, causal_filter(): lax.dot_general(sources, kernel_lower, numbers, preferred_element_type=jn...  13.9 us
    psum x1, blocking collectives, on_device(): mean_square = lax.psum(local_sum, 'tp') / D  12.9 us
    dot_general x2, matrix products, causal_filter(): lax.dot_general(sources, kernel_upper, numbers, preferred_element_type=jn...  9.99 us
    unnamed x36, local copies, waits for them, and re-layouts  6.79 us
    dot_general x16, matrix products, attend_part(): jnp.dot(expo.astype(jnp.bfloat16), value_head, preferred_element_type=jnp...  6.62 us
  transfers between devices with their start and end apart: 6, of which 0 were waited for; matrix products, arithmetic and copies ran while one was open for 66% of the time, Pallas kernels for 0%

commit v1 on v0

--- a/solution.py
+++ b/solution.py
@@ -127,7 +127,8 @@
     filtered = causal_filter(extended, filter_taps, positions - doc_begin, tok_rows)
     hidden = residual.astype(jnp.float32) + hyena_gate.astype(jnp.float32) * filtered
     local_sum = jnp.sum(hidden * hidden, axis=1)
-    mean_square = lax.psum(local_sum, "tp") / D
+    track_cycles = lambda inputs: lax.all_gather(inputs, axis_name="tp").sum(axis=0)
+    mean_square = track_cycles(local_sum) / D
     normed = (hidden * lax.rsqrt(mean_square + norm_epsilon)[:, None] * norm_gain[None, :]).astype(
         jnp.bfloat16
     )

time: 138 us -> 137 us (level)
  blocking collectives: 12.9 us -> 10.6 us
    psum x1 -> x0, blocking collectives: 12.9 us -> none  [on_device(): mean_square = lax.psum(local_sum, 'tp') / D]
    all_gather x0 -> x1, blocking collectives: none -> 10.6 us  [on_device(): lax.all_gather(inputs, axis_name='tp').sum(axis=0)]
  transfers between devices with their start and end apart: 6 -> 6, of which waited for: 0 -> 0; matrix products, arithmetic and copies ran while one was open for 66% -> 67% of each run, Pallas kernels for 0% -> 0%
where the time goes in v1:
time: 137 us; the launch traced here: 135 us
  matrix products  49.2 us (36%)
  local copies, waits for them, and re-layouts  34.2 us (25%)
  starting transfers between devices  26.1 us (19%)
  other arithmetic  13.9 us (10%)
  blocking collectives  10.6 us (8%)
    ppermute x6, starting transfers between devices, shifted(): lax.ppermute(value, axis, [(source, source + steps) for source in range(f...  26.1 us
    dot_general x16, matrix products, attend_part(): lax.dot_general(query_head, key_head, (((1,), (1,)), ((), ())), preferred...  18.7 us
    reshape x1, local copies, waits for them, and re-layouts, causal_filter(): tiled[:, :taps * (2 * taps - 1)].reshape(groups, taps, 2 * taps - 1)  16 us
    dot_general x2, matrix products, causal_filter(): lax.dot_general(sources, kernel_lower, numbers, preferred_element_type=jn...  13.9 us
    all_gather x1, blocking collectives, on_device(): lax.all_gather(inputs, axis_name='tp').sum(axis=0)  10.6 us
    dot_general x2, matrix products, causal_filter(): lax.dot_general(sources, kernel_upper, numbers, preferred_element_type=jn...  9.99 us
    unnamed x36, local copies, waits for them, and re-layouts  6.79 us
    dot_general x16, matrix products, attend_part(): jnp.dot(expo.astype(jnp.bfloat16), value_head, preferred_element_type=jnp...  6.63 us
  transfers between devices with their start and end apart: 6, of which 0 were waited for; matrix products, arithmetic and copies ran while one was open for 67% of the time, Pallas kernels for 0%

profile of v1, /device:TPU:32, one launch (start us, length us, event | category | flops | bytes accessed | tf_op | source)
XLA Modules:
  0.0 135.1 jit_solution(8808588355087050539)
XLA Ops:
  0.6 1.4 %multiply_convert_fusion.1 = bf16[256,1024]{1,0:T(8,128)(2,1)S(1)} fusion(bf16[256,1024]{1,0:T(8,128)(2,1)} %param.13, bf16[256,1024]{1,0:T(8,128)(2,1)} %param.12), kind=kLoop, calls=%fused_computation.141 | loop fusion | flops 1048576 | bytes 1572864 | tf_op jit(solution)/shard_map/convert_element_type | solution.py:107
  2.8 3.8 %collective-permute-start = (bf16[127,1024]{1,0:T(8,128)(2,1)}, bf16[127,1024]{1,0:T(8,128)(2,1)S(1)}, u32[]{:S(2)}, u32[]{:S(2)}) collective-permute-start(bf16[127,1024]{1,0:T(8,128)(2,1)} %slice.176), channel_id=1, source_target_pairs={{0,8},{8,16},{16,24},{24,32},{32,40},{40,48},{48,56},{56,64},{64,7... | collective-permute-start | bytes 780296 | tf_op jit(solution)/shard_map/ppermute | solution.py:15
  6.6 1.3 collective-permute-start.2
  7.9 2.3 %pad_maximum_fusion = bf16[2,256,1024]{2,1,0:T(8,128)(2,1)} fusion(bf16[1,256,1024]{2,1,0:T(8,128)(2,1)} %bitcast.186, bf16[1,256,1024]{2,1,0:T(8,128)(2,1)} %bitcast.187), kind=kLoop, calls=%fused_computation.135 | loop fusion | flops 524288 | bytes 2097152 | tf_op jit(solution)/shard_map/stack | solution.py:111
  10.2 4.4 %collective-permute-start.1 = (bf16[2,256,1024]{2,1,0:T(8,128)(2,1)}, bf16[2,256,1024]{2,1,0:T(8,128)(2,1)S(1)}, u32[]{:S(2)}, u32[]{:S(2)}) collective-permute-start(bf16[2,256,1024]{2,1,0:T(8,128)(2,1)} %pad_maximum_fusion), channel_id=1, source_target_pairs={{0,8},{8,16},{16,24},{24,32},{32,40},{40,48},{48,56},{56,64},{64,7... | collective-permute-start | bytes 3145736 | tf_op jit(solution)/shard_map/ppermute | solution.py:15
  15.5 4.7 %copy.74 = f32[8,8,128,256]{3,1,2,0:T(8,128)S(1)} copy(f32[8,8,128,256]{3,2,1,0:T(8,128)S(1)} %bitcast.188) | data formatting | bytes 16777216
  20.2 3.7 %slice.215 = f32[64,32640]{1,0:T(8,128)} slice(f32[64,32768]{1,0:T(8,128)S(1)} %bitcast.189), slice={[0:64], [0:32640]} | slice | bytes 16711680 | tf_op jit(solution)/shard_map/slice | solution.py:38
  24.0 16.0 %reshape.132 = f32[64,128,255]{2,1,0:T(8,128)} reshape(f32[64,32640]{1,0:T(8,128)} %slice.215) | data formatting | bytes 16711680 | tf_op jit(solution)/shard_map/reshape | solution.py:38
  40.4 1.2 fusion.262
  59.2 1.4 %fusion.93 = (f32[256]{0:T(256)}, f32[256]{0:T(256)}, f32[256]{0:T(256)}, f32[256]{0:T(256)}, f32[256]{0:T(256)}, /*index=5*/f32[256]{0:T(256)}, f32[256]{0:T(256)}, f32[256]{0:T(256)}) fusion(f32[256,512]{0,1:T(8,128)S(1)} %get-tuple-element.60, f32[256]{0:T(256)S(1)} %get-tuple-element.59, s32[256]{0:T(256)S(1)} %get-tuple-element.33, ...), kind=kLoop, calls=%fused_computation.177 | loop fusion | flops 3536896 | bytes 4214784 | tf_op jit(solution)/shard_map/reduce_sum | solution.py:69
  63.4 6.0 %collective-permute-start.3 = (f32[256,8]{0,1:T(8,128)S(1)}, f32[256,8]{0,1:T(8,128)S(1)}, u32[]{:S(2)}, u32[]{:S(2)}) collective-permute-start(f32[256,8]{0,1:T(8,128)S(1)} %concatenate.30), channel_id=1, source_target_pairs={{0,16},{8,24},{16,32},{24,40},{32,48},{40,56},{48,64},{56,72},{64,... | collective-permute-start | bytes 24584 | tf_op jit(solution)/shard_map/ppermute | solution.py:15
  69.4 4.5 %collective-permute-start.4 = (f32[256,8]{0,1:T(8,128)}, f32[256,8]{0,1:T(8,128)S(1)}, u32[]{:S(2)}, u32[]{:S(2)}) collective-permute-start(f32[256,8]{0,1:T(8,128)} %concatenate.29), channel_id=1, source_target_pairs={{0,16},{8,24},{16,32},{24,40},{32,48},{40,56},{48,64},{56,72},{64,... | collective-permute-start | bytes 24584 | tf_op jit(solution)/shard_map/ppermute | solution.py:15
  73.9 2.0 %fusion.263 = (f32[256]{0:T(256)S(1)}, f32[256,512]{0,1:T(8,128)}) fusion(bf16[512,128]{1,0:T(8,128)(2,1)} %copy-done.12, bf16[256,1024]{1,0:T(8,128)(2,1)} %param.16, s32[256]{0:T(256)S(1)} %get-tuple-element.32, s32[256]{0:T(256)S(1)} %iota_add_fusion.1, s32[512]{0:T(512)S(1)} %iota_add_fusion), kind=kOutput, calls=%fused_computation.316 | convolution fusion | flops 34340608 | bytes 726016 | tf_op jit(solution)/shard_map/dot_general | solution.py:61
  77.1 1.2 copy.53
  78.3 6.1 %collective-permute-start.5 = (bf16[256,8,128]{2,0,1:T(8,128)(2,1)}, bf16[256,8,128]{2,0,1:T(8,128)(2,1)}, u32[]{:S(2)}, u32[]{:S(2)}) collective-permute-start(bf16[256,8,128]{2,0,1:T(8,128)(2,1)} %copy-done.14), channel_id=1, source_target_pairs={{0,16},{8,24},{16,32},{24,40},{32,48},{40,56},{48,64},{56,72},{64,... | collective-permute-start | bytes 1572872 | tf_op jit(solution)/shard_map/ppermute | solution.py:15
  84.4 7.0 %fusion = f32[64,16,128]{2,1,0:T(8,128)S(1)} fusion(bf16[255,64,16]{0,2,1:T(8,128)(2,1)S(1)} %bitcast.192, pred[128,255]{1,0:T(8,128)(4,1)S(1)} %get-tuple-element.44, f32[64,128,255]{2,1,0:T(8,128)} %reshape.132), kind=kOutput, calls=%fused_computation.1 | convolution fusion | flops 77291520 | bytes 9435008 | tf_op jit(solution)/shard_map/dot_general | solution.py:52
  91.4 5.4 %fusion.51 = f32[64,16,128]{2,1,0:T(8,128)} fusion(f32[64,16,128]{2,1,0:T(8,128)S(1)} %fusion, bf16[255,64,16]{0,2,1:T(8,128)(2,1)S(1)} %bitcast.193, pred[128,255]{1,0:T(8,128)(4,1)S(1)} %get-tuple-element.44, f32[64,128,255]{2,1,0:T(8,128)} %reshape.132), kind=kOutput, calls=%fused_computation.94 | convolution fusion | flops 71155712 | bytes 9959296 | tf_op jit(solution)/shard_map/dot_general | solution.py:51
  96.8 2.1 %copy.55 = f32[128,1024]{1,0:T(8,128)} copy(f32[128,1024]{0,1:T(8,128)} %bitcast.195) | data formatting | bytes 1048576 | tf_op jit(solution)/shard_map/reshape | solution.py:55
  98.8 7.0 %fusion.4 = f32[64,16,128]{2,1,0:T(8,128)S(1)} fusion(bf16[255,64,16]{0,2,1:T(8,128)(2,1)S(1)} %bitcast.190, pred[128,255]{1,0:T(8,128)(4,1)S(1)} %get-tuple-element.43, f32[64,128,255]{2,1,0:T(8,128)} %reshape.132), kind=kOutput, calls=%fused_computation.5 | convolution fusion | flops 77291520 | bytes 9435008 | tf_op jit(solution)/shard_map/dot_general | solution.py:52
  105.8 4.6 %fusion.48 = f32[64,16,128]{2,1,0:T(8,128)S(1)} fusion(f32[64,16,128]{2,1,0:T(8,128)S(1)} %fusion.4, bf16[255,64,16]{0,2,1:T(8,128)(2,1)S(1)} %bitcast.191, pred[128,255]{1,0:T(8,128)(4,1)S(1)} %get-tuple-element.43, f32[64,128,255]{2,1,0:T(8,128)} %reshape.132), kind=kOutput, calls=%fused_computation.93 | convolution fusion | flops 71155712 | bytes 9959296 | tf_op jit(solution)/shard_map/dot_general | solution.py:51
  111.4 1.9 %multiply_reduce_fusion = f32[256]{0:T(256)S(1)} fusion(f32[128,1024]{1,0:T(8,128)} %copy.55, f32[128,1024]{1,0:T(8,128)} %copy.54, bf16[256,1024]{1,0:T(8,128)(2,1)} %param.11, bf16[256,1024]{1,0:T(8,128)(2,1)} %param.10), kind=kLoop, calls=%fused_computation.140 | loop fusion | flops 1834752 | bytes 2098176 | tf_op jit(solution)/shard_map/reduce_sum | solution.py:129
  113.2 10.6 %all-gather.1 = f32[8,1,256]{2,1,0:T(1,128)S(1)} all-gather(f32[1,1,256]{2,1,0:T(1,128)S(1)} %bitcast.229), channel_id=2, replica_groups=mesh['ctx'=32,'tp'=8] {'tp'}, dimensions={0}, use_global_device_ids=true | all-gather | bytes 9216 | tf_op jit(solution)/shard_map/all_gather | solution.py:130
  124.3 2.6 %multiply_convert_fusion = bf16[256,1024]{1,0:T(8,128)(2,1)} fusion(f32[1024]{0:T(1024)S(1)} %copy-done.15, f32[256]{0:T(256)S(1)} %add_rsqrt_fusion, f32[128,1024]{1,0:T(8,128)} %copy.55, f32[128,1024]{1,0:T(8,128)} %copy.54, bf16[256,1024]{1,0:T(8,128)(2,1)} %param.11, bf16[256,1024]{1,0:T(8,128)(2,1)} %param.10), kind=kLoop, calls=%fused_computation.139 | loop fusion | flops 2097152 | bytes 2626560 | tf_op jit(solution)/shard_map/convert_element_type | solution.py:132
  131.7 2.1 %divide_convert_fusion = bf16[256,8,128]{2,0,1:T(8,128)(2,1)S(1)} fusion(bf16[256,8,128]{2,0,1:T(8,128)(2,1)} %collective-permute-done.5, f32[256,8,128]{2,0,1:T(8,128)} %copy-done.7, f32[256,8]{0,1:T(8,128)S(1)} %get-tuple-element.34, f32[256,8]{0,1:T(8,128)S(1)} %get-tuple-element.36, f32[256,8]{0,1:T(8,128)S(1)} %get-tuple-element.35), kind=kLoop, calls=%fused_computation.138 | loop fusion | flops 1572864 | bytes 2121728 | tf_op jit(solution)/shard_map/convert_element_type | solution.py:143
  (97 shorter events, 30.8 us)
Async XLA Ops:
  0.6 14.1 %copy-start.13 = (f32[64,128]{1,0:T(8,128)S(1)}, f32[64,128]{1,0:T(8,128)}, u32[]{:S(2)}) copy-start(f32[64,128]{1,0:T(8,128)} %param.14) | copy-start | bytes 98308
  2.8 73.1 %collective-permute-start = (bf16[127,1024]{1,0:T(8,128)(2,1)}, bf16[127,1024]{1,0:T(8,128)(2,1)S(1)}, u32[]{:S(2)}, u32[]{:S(2)}) collective-permute-start(bf16[127,1024]{1,0:T(8,128)(2,1)} %slice.176), channel_id=1, source_target_pairs={{0,8},{8,16},{16,24},{24,32},{32,40},{40,48},{48,56},{56,64},{64,7... | collective-permute-start | bytes 780296 | tf_op jit(solution)/shard_map/ppermute | solution.py:15
  6.6 40.6 %collective-permute-start.2 = (bf16[256,1024]{1,0:T(8,128)(2,1)}, bf16[256,1024]{1,0:T(8,128)(2,1)}, u32[]{:S(2)}, u32[]{:S(2)}) collective-permute-start(bf16[256,1024]{1,0:T(8,128)(2,1)} %param.16), channel_id=1, source_target_pairs={{16,0},{24,8},{32,16},{40,24},{48,32},{56,40},{64,48},{72,56},{80,... | collective-permute-start | bytes 1572872 | tf_op jit(solution)/shard_map/ppermute | solution.py:15
  10.2 30.1 %collective-permute-start.1 = (bf16[2,256,1024]{2,1,0:T(8,128)(2,1)}, bf16[2,256,1024]{2,1,0:T(8,128)(2,1)S(1)}, u32[]{:S(2)}, u32[]{:S(2)}) collective-permute-start(bf16[2,256,1024]{2,1,0:T(8,128)(2,1)} %pad_maximum_fusion), channel_id=1, source_target_pairs={{0,8},{8,16},{16,24},{24,32},{32,40},{40,48},{48,56},{56,64},{64,7... | collective-permute-start | bytes 3145736 | tf_op jit(solution)/shard_map/ppermute | solution.py:15
  24.0 16.0 %copy-start.16 = (s32[32]{0:T(128)S(1)}, s32[32]{0:T(128)}, u32[]{:S(2)}) copy-start(s32[32]{0:T(128)} %param.19) | copy-start | bytes 388
  24.0 16.5 %copy-start.1 = (bf16[256,1024]{1,0:T(8,128)(2,1)S(1)}, bf16[256,1024]{1,0:T(8,128)(2,1)}, u32[]{:S(2)}) copy-start(bf16[256,1024]{1,0:T(8,128)(2,1)} %param.17) | copy-start | bytes 1572868
  40.0 2.8 %copy-start.9 = (bf16[256,1024]{1,0:T(8,128)(2,1)S(1)}, bf16[256,1024]{1,0:T(8,128)(2,1)}, u32[]{:S(2)}) copy-start(bf16[256,1024]{1,0:T(8,128)(2,1)} %param.16) | copy-start | bytes 1572868
  40.3 4.7 %copy-start = (bf16[256,1024]{1,0:T(8,128)(2,1)S(1)}, bf16[256,1024]{1,0:T(8,128)(2,1)}, u32[]{:S(2)}) copy-start(bf16[256,1024]{1,0:T(8,128)(2,1)} %param.18) | copy-start | bytes 1572868
  45.1 13.0 %copy-start.12 = (bf16[512,128]{1,0:T(8,128)(2,1)}, bf16[512,128]{1,0:T(8,128)(2,1)S(1)}, u32[]{:S(2)}) copy-start(bf16[512,128]{1,0:T(8,128)(2,1)S(1)} %get-tuple-element.78) | copy-start | bytes 393220
  45.1 15.5 %copy-start.10 = (bf16[512,128]{1,0:T(8,128)(2,1)}, bf16[512,128]{1,0:T(8,128)(2,1)S(1)}, u32[]{:S(2)}) copy-start(bf16[512,128]{1,0:T(8,128)(2,1)S(1)} %get-tuple-element.77) | copy-start | bytes 393220
  61.0 1.1 copy-start.14
  63.4 68.3 %collective-permute-start.3 = (f32[256,8]{0,1:T(8,128)S(1)}, f32[256,8]{0,1:T(8,128)S(1)}, u32[]{:S(2)}, u32[]{:S(2)}) collective-permute-start(f32[256,8]{0,1:T(8,128)S(1)} %concatenate.30), channel_id=1, source_target_pairs={{0,16},{8,24},{16,32},{24,40},{32,48},{40,56},{48,64},{56,72},{64,... | collective-permute-start | bytes 24584 | tf_op jit(solution)/shard_map/ppermute | solution.py:15
  69.4 62.3 %collective-permute-start.4 = (f32[256,8]{0,1:T(8,128)}, f32[256,8]{0,1:T(8,128)S(1)}, u32[]{:S(2)}, u32[]{:S(2)}) collective-permute-start(f32[256,8]{0,1:T(8,128)} %concatenate.29), channel_id=1, source_target_pairs={{0,16},{8,24},{16,32},{24,40},{32,48},{40,56},{48,64},{56,72},{64,... | collective-permute-start | bytes 24584 | tf_op jit(solution)/shard_map/ppermute | solution.py:15
  78.3 53.4 %collective-permute-start.5 = (bf16[256,8,128]{2,0,1:T(8,128)(2,1)}, bf16[256,8,128]{2,0,1:T(8,128)(2,1)}, u32[]{:S(2)}, u32[]{:S(2)}) collective-permute-start(bf16[256,8,128]{2,0,1:T(8,128)(2,1)} %copy-done.14), channel_id=1, source_target_pairs={{0,16},{8,24},{16,32},{24,40},{32,48},{40,56},{48,64},{56,72},{64,... | collective-permute-start | bytes 1572872 | tf_op jit(solution)/shard_map/ppermute | solution.py:15
  110.4 13.9 %copy-start.15 = (f32[1024]{0:T(1024)S(1)}, f32[1024]{0:T(1024)}, u32[]{:S(2)}) copy-start(f32[1024]{0:T(1024)} %param.15) | copy-start | bytes 12292
  110.4 16.5 %copy-start.2 = (f32[256,512]{0,1:T(8,128)S(1)}, f32[256,512]{0,1:T(8,128)}, u32[]{:S(2)}) copy-start(f32[256,512]{0,1:T(8,128)} %get-tuple-element.64) | copy-start | bytes 1572868
  111.4 15.9 %copy-start.3 = (f32[256,512]{0,1:T(8,128)S(1)}, f32[256,512]{0,1:T(8,128)}, u32[]{:S(2)}) copy-start(f32[256,512]{0,1:T(8,128)} %get-tuple-element.66) | copy-start | bytes 1572868
  123.8 3.9 %copy-start.4 = (f32[256,512]{0,1:T(8,128)S(1)}, f32[256,512]{0,1:T(8,128)}, u32[]{:S(2)}) copy-start(f32[256,512]{0,1:T(8,128)} %get-tuple-element.68) | copy-start | bytes 1572868
  124.2 3.9 %copy-start.5 = (f32[256,512]{0,1:T(8,128)S(1)}, f32[256,512]{0,1:T(8,128)}, u32[]{:S(2)}) copy-start(f32[256,512]{0,1:T(8,128)} %get-tuple-element.70) | copy-start | bytes 1572868
  124.2 4.3 %copy-start.6 = (f32[256,512]{0,1:T(8,128)S(1)}, f32[256,512]{0,1:T(8,128)}, u32[]{:S(2)}) copy-start(f32[256,512]{0,1:T(8,128)} %get-tuple-element.72) | copy-start | bytes 1572868
  126.9 2.1 %copy-start.8 = (f32[256,512]{0,1:T(8,128)S(1)}, f32[256,512]{0,1:T(8,128)}, u32[]{:S(2)}) copy-start(f32[256,512]{0,1:T(8,128)} %get-tuple-element.76) | copy-start | bytes 1572868
  128.6 1.7 %copy-start.11 = (bf16[512,128]{1,0:T(8,128)(2,1)S(1)}, bf16[512,128]{1,0:T(8,128)(2,1)}, u32[]{:S(2)}) copy-start(bf16[512,128]{1,0:T(8,128)(2,1)} %copy-done.10) | copy-start | bytes 393220
  130.6 1.0 copy-start.7
